TPU v7x, 32 devices: a whole 2x2x4 slice. The times are simulated.
32 devices in a mesh: fsdp: 4 (over y, x), seq: 8 (over z, core).
Axes of the slice: x: 2, y: 2, z: 4, core: 2. Of those that a mesh axis runs over, the one named last changes fastest.
Arguments:
- events: bfloat16 [4, 1024, 2048], P('fsdp', 'seq'), may hold values from -6 to 6
- type_ids: int32 [4, 1024], P('fsdp', 'seq'), may hold values from 0 to 255
- type_table: bfloat16 [256, 2048], P('fsdp'), may hold values from -6 to 6
- norm_gain: float32 [2048], replicated, may hold values from 0.25 to 1.75
- kernel: bfloat16 [2048, 1152], P('fsdp'), may hold values from -0.1875 to 0.1875
- upstream: bfloat16 [4, 1024, 2048], P('fsdp', 'seq'), may hold values from -6 to 6
Outputs:
- input_grad: bfloat16 [4, 1024, 2048], P('fsdp', 'seq')
- table_grad: float32 [256, 2048], P(('fsdp', 'seq'))
- gain_grad: float32 [2048], P(('fsdp', 'seq'))
- kernel_grad: float32 [2048, 1152], P('seq')
All inputs are finite; a program needn't handle non-finite values.
Results may differ from a plain program's by a relative error of at most 0.0053.
Values may be sent and summed in bfloat16 or wider, within the bound.
No kernel may reach another device: no remote copies, remote signals or barrier semaphores. Data moves between devices by JAX's collectives and lax.ppermute only.
A program may use at most 128 MiB of HBM per device.

v0:
```python
import jax
import jax.numpy as jnp
from jax import lax
from jax.sharding import PartitionSpec as P

GROUPS = 16
KERNEL = 9


def with_halo(cells, sides, width):
    for axis, dim in sides:
        count = lax.axis_size(axis)
        ends = count - 1
        head = lax.slice_in_dim(cells, 0, width, axis=dim)
        tail = lax.slice_in_dim(cells, cells.shape[dim] - width, cells.shape[dim], axis=dim)
        cells = jnp.concatenate(
            [
                lax.ppermute(tail, axis, [(i, (i + 1) % count) for i in range(ends)]),
                cells,
                lax.ppermute(head, axis, [((i + 1) % count, i) for i in range(ends)]),
            ],
            axis=dim,
        )
    return cells


def from_partner(value, axis, apart):
    mask = 2**apart
    pairs = [(source, source ^ mask) for source in range(lax.axis_size(axis))]
    return lax.ppermute(value, axis, pairs)


def body(events, type_ids, type_table, norm_gain, kernel, upstream):
    length = events.shape[1]
    width = events.shape[2]
    chans = width // GROUPS
    half = KERNEL // 2
    seq_count = lax.axis_size("seq")
    total = length * seq_count * lax.axis_size("fsdp")
    scale = 1.0 / jnp.sqrt(jnp.float32(total))
    table = lax.all_gather(type_table, "fsdp", axis=0, tiled=True)
    onehot = (type_ids[0][:, None] == jnp.arange(table.shape[0], dtype=jnp.int32)[None, :]).astype(
        jnp.bfloat16
    )
    mixed = events[0].astype(jnp.float32) + jnp.dot(
        onehot, table, preferred_element_type=jnp.float32
    )
    inv = lax.rsqrt(jnp.mean(mixed * mixed, axis=-1, keepdims=True) + 1e-06)
    normed = (mixed * inv * norm_gain).astype(jnp.bfloat16)
    padded = with_halo(normed, (("seq", 0),), half)
    padded = padded.reshape(length + 2 * half, GROUPS, chans)
    weights = lax.all_gather(kernel, "fsdp", axis=0, tiled=True).reshape(
        GROUPS, chans, KERNEL, chans
    )
    conv = jnp.zeros((length, GROUPS, chans), jnp.float32)
    for k in range(KERNEL):
        conv = conv + jnp.einsum(
            "tgc,goc->tgo",
            padded[k : k + length],
            weights[:, :, k, :],
            preferred_element_type=jnp.float32,
        )
    up_float = upstream[0].astype(jnp.float32)
    sig = jax.nn.sigmoid(conv)
    dconv = (up_float.reshape(length, GROUPS, chans) * sig * (1.0 + conv * (1.0 - sig))).astype(
        jnp.bfloat16
    )
    dflat = dconv.reshape(length, width)
    dpad = with_halo(dflat, (("seq", 0),), half)
    dpad = dpad.reshape(length + 2 * half, GROUPS, chans)
    dnormed = jnp.zeros((length, GROUPS, chans), jnp.float32)
    for k in range(KERNEL):
        dnormed = dnormed + jnp.einsum(
            "tgo,goc->tgc",
            dpad[2 * half - k : 2 * half - k + length],
            weights[:, :, k, :],
            preferred_element_type=jnp.float32,
        )
    slice_width = width // seq_count
    normed_slice, dconv_slice = (
        lax.all_to_all(normed, "seq", split_axis=1, concat_axis=0, tiled=True),
        lax.all_to_all(dflat, "seq", split_axis=1, concat_axis=0, tiled=True),
    )
    whole = normed_slice.shape[0]
    if slice_width < chans:
        spread = chans // slice_width
        position = lax.axis_index("seq")
        group_rows = normed_slice
        for bit in range(spread.bit_length() - 1):
            partner = from_partner(group_rows, "seq", bit)
            lower = position >> bit & 1 == 0
            group_rows = jnp.where(
                lower,
                jnp.concatenate([group_rows, partner], axis=1),
                jnp.concatenate([partner, group_rows], axis=1),
            )
        group_in = group_rows.reshape(whole, 1, chans)
        group_out = dconv_slice.reshape(whole, 1, slice_width)
    else:
        local_groups = slice_width // chans
        group_in = normed_slice.reshape(whole, local_groups, chans)
        group_out = dconv_slice.reshape(whole, local_groups, chans)
    group_pad = jnp.pad(group_in, ((half, half), (0, 0), (0, 0)))
    kterms = []
    for k in range(KERNEL):
        kterms.append(
            jnp.einsum(
                "tgo,tgc->goc",
                group_out,
                group_pad[k : k + whole],
                preferred_element_type=jnp.float32,
            )
        )
    kernel_part = jnp.stack(kterms, axis=2).reshape(slice_width, KERNEL * chans) * scale
    kernel_grad = lax.psum(kernel_part, "fsdp")
    dnormed = dnormed.reshape(length, width)
    gain_term = jnp.sum(dnormed * mixed * inv, axis=0) * scale
    scaled = norm_gain * dnormed
    dmixed = inv * scaled - mixed * inv * inv * inv * jnp.mean(
        scaled * mixed, axis=-1, keepdims=True
    )
    input_grad = (up_float + dmixed).astype(jnp.bfloat16)
    table_term = (
        lax.dot_general(
            onehot, input_grad, (((0,), (0,)), ((), ())), preferred_element_type=jnp.float32
        )
        * scale
    )
    table_grad, gain_grad = (
        lax.psum_scatter(table_term, ("fsdp", "seq"), scatter_dimension=0, tiled=True),
        lax.psum_scatter(gain_term, ("fsdp", "seq"), scatter_dimension=0, tiled=True),
    )
    return (input_grad[None], table_grad, gain_grad, kernel_grad)


def solution(mesh):
    return jax.shard_map(
        body,
        mesh=mesh,
        in_specs=(
            P("fsdp", "seq", None),
            P("fsdp", "seq"),
            P("fsdp", None),
            P(),
            P("fsdp", None),
            P("fsdp", "seq", None),
        ),
        out_specs=(
            P("fsdp", "seq", None),
            P(("fsdp", "seq"), None),
            P(("fsdp", "seq")),
            P("seq", None),
        ),
        check_vma=False,
    )
```

profile of v0, /device:TPU:0, one launch (start us, length us, event | category | flops | bytes accessed | tf_op | source)
XLA Modules:
  0.0 384.2 jit_solution(598750002941307094)
XLA Ops:
  7.2 0.7 all-gather.3.cloned.1.call-update
  8.0 0.7 all-gather.5.cloned.1.call-update
  8.7 30.6 %all-gather.3.cloned.1.call-done = bf16[256,2048]{1,0:T(8,128)(2,1)} async-done(((bf16[64,2048]{1,0:T(8,128)(2,1)}), bf16[256,2048]{1,0:T(8,128)(2,1)}) %all-gather.3.cloned.1.call-update) | async-done | bytes 1048592 | tf_op jit(solution)/shard_map/all_gather | solution.py:41
  39.2 1.7 multiply_reduce_fusion.2
  41.1 1.0 copy.192
  42.1 4.6 %all-to-all-start.1 = ((bf16[128,8,256]{0,2,1:T(8,128)(2,1)}), bf16[128,8,256]{0,2,1:T(8,128)(2,1)S(1)}, u32[]{:S(2)}, u32[]{:S(2)}) async-start(bf16[128,8,256]{0,2,1:T(8,128)(2,1)} %bitcast.30), calls=%async_computation.2 | async-start | bytes 1048576 | tf_op jit(solution)/shard_map/all_to_all | solution.py:81
  46.7 2.4 collective-permute-start
  49.1 1.3 collective-permute-start.1
  50.6 1.2 copy.213
  51.7 1.6 collective-permute-done.1
  53.4 2.7 fusion.52
  56.0 6.0 %all-to-all-done.1 = bf16[128,8,256]{0,2,1:T(8,128)(2,1)S(1)} async-done(((bf16[128,8,256]{0,2,1:T(8,128)(2,1)}), bf16[128,8,256]{0,2,1:T(8,128)(2,1)S(1)}, u32[]{:S(2)}, u32[]{:S(2)}) %all-to-all-start.1) | async-done | bytes 524320 | tf_op jit(solution)/shard_map/all_to_all | solution.py:81
  62.6 1.0 copy.169
  63.7 34.5 %all-gather.5.cloned.1.call-done = bf16[2048,1152]{1,0:T(8,128)(2,1)} async-done(((bf16[512,1152]{1,0:T(8,128)(2,1)}), bf16[2048,1152]{1,0:T(8,128)(2,1)}) %all-gather.5.cloned.1.call-update) | async-done | bytes 4718608 | tf_op jit(solution)/shard_map/all_gather | solution.py:52
  98.2 10.5 %reshape.88 = bf16[16,128,9,128]{3,2,1,0:T(8,128)(2,1)} reshape(bf16[2048,1152]{1,0:T(8,128)(2,1)} %all-gather.5.cloned.1.call-done) | data formatting | bytes 9437184 | tf_op jit(solution)/shard_map/reshape | solution.py:52
  108.6 19.8 %fusion.82 = (bf16[16,128,1,128]{3,2,1,0:T(2,128)(2,1)S(1)}, bf16[16,128,1,128]{3,2,1,0:T(2,128)(2,1)S(1)}, bf16[16,128,1,128]{3,2,1,0:T(2,128)(2,1)S(1)}, bf16[...) fusion(bf16[16,128,9,128]{3,2,1,0:T(8,128)(2,1)} %reshape.88), kind=kLoop, calls=%fused_computation.154 | loop fusion | bytes 9437184 | tf_op jit(solution)/shard_map/slice | solution.py:60
  129.0 0.9 copy-done.22
  130.5 0.9 copy-done.21
  131.8 0.7 copy-done.20
  136.1 0.7 copy-done.25
  137.0 0.8 fusion.14
  137.9 1.1 copy.145
  138.9 1.3 collective-permute-start.2
  140.2 1.1 copy.155
  141.3 3.8 collective-permute-start.3
  145.1 2.7 fusion.63
  147.8 1.0 copy.144
  148.8 4.7 %all-to-all-start = ((bf16[128,8,256]{0,2,1:T(8,128)(2,1)}), bf16[128,8,256]{0,2,1:T(8,128)(2,1)S(1)}, u32[]{:S(2)}, u32[]{:S(2)}) async-start(bf16[128,8,256]{0,2,1:T(8,128)(2,1)} %bitcast.28), calls=%async_computation.1 | async-start | bytes 1048576 | tf_op jit(solution)/shard_map/all_to_all | solution.py:82
  153.7 6.9 %pad_maximum_fusion = (bf16[128,2048]{0,1:T(8,128)(2,1)S(1)}, bf16[128,2048]{0,1:T(8,128)(2,1)S(1)}, bf16[128,2048]{0,1:T(8,128)(2,1)S(1)}, bf16[128,2048]{0,1:T...) fusion(bf16[128,2048]{0,1:T(8,128)(2,1)} %bitcast.13, ...), kind=kLoop, calls=%fused_computation.105 | loop fusion | flops 8388608 | bytes 4751360 | tf_op jit(solution)/shard_map/concatenate | solution.py:16
  161.0 0.8 copy-done.7
  162.2 0.9 copy-done.5
  163.4 0.9 copy-done.12
  165.0 0.9 copy-done.3
  166.2 0.9 copy-done.1
  167.8 0.8 copy-done.15
  168.6 1.3 convolution_add_fusion.1
  170.0 1.6 copy.191
  171.5 1.1 copy.166
  172.7 1.3 reshape.83
  174.0 1.4 fusion.10
  178.0 1.9 copy.171
  180.0 2.4 copy.284
  182.7 0.7 copy-done.17
  183.8 1.9 convolution_multiply_fusion
  185.7 39.9 %all-reduce.1 = f32[2048]{0:T(1024)S(1)} all-reduce(f32[2048]{0:T(1024)S(1)} %broadcast_multiply_fusion.1), channel_id=3, replica_groups=mesh['fsdp'=4,'seq'=8] {'fsdp','seq'}, use_global_device_ids=true, to_apply=%region_4.5.clone | all-reduce | flops 2048 | bytes 16384
  226.2 11.7 %all-reduce.4.cloned.1.call-done = f32[256,1152]{0,1:T(8,128)} async-done(((f32[256,1152]{0,1:T(8,128)}), f32[256,1152]{0,1:T(8,128)}) %all-reduce.4.cloned.1.call-update) | async-done | bytes 1179664 | tf_op jit(solution)/shard_map/psum | solution.py:115
  237.9 2.7 copy.172
  240.6 137.1 %reduce-scatter.2.cloned.1.call-done = f32[8,2048]{1,0:T(8,128)} async-done(((f32[256,2048]{1,0:T(8,128)}), f32[8,2048]{1,0:T(8,128)}) %reduce-scatter.2.cloned.1.call-update) | async-done | bytes 65552 | tf_op jit(solution)/shard_map/reduce_scatter | solution.py:130
  (97 shorter events, 13.1 us)
Async XLA Ops:
  7.2 32.1 %copy-start.30 = (s32[1,128]{1,0:T(1,128)S(1)}, s32[1,128]{1,0:T(1,128)}, u32[]{:S(2)}) copy-start(s32[1,128]{1,0:T(1,128)} %param.7) | copy-start | bytes 1540
  7.2 32.1 %copy-start.26 = (bf16[1,128,2048]{2,1,0:T(8,128)(2,1)S(1)}, bf16[1,128,2048]{2,1,0:T(8,128)(2,1)}, u32[]{:S(2)}) copy-start(bf16[1,128,2048]{2,1,0:T(8,128)(2,1)} %param.6) | copy-start | bytes 1572868
  7.2 32.0 %all-gather.3.cloned.1.call-start = ((), (), s32[]{:S(2)}) async-start(), calls=%async_computation.3 | async-start | bytes 1310720 | tf_op jit(solution)/shard_map/all_gather | solution.py:41
  7.9 90.2 %all-gather.5.cloned.1.call-start = ((), (), s32[]{:S(2)}) async-start(), calls=%async_computation.4 | async-start | bytes 5898240 | tf_op jit(solution)/shard_map/all_gather | solution.py:52
  39.2 1.7 copy-start.29
  41.1 9.4 %copy-start.16 = (bf16[1,128,2048]{2,1,0:T(8,128)(2,1)S(1)}, bf16[1,128,2048]{2,1,0:T(8,128)(2,1)}, u32[]{:S(2)}) copy-start(bf16[1,128,2048]{2,1,0:T(8,128)(2,1)} %param.11) | copy-start | bytes 1572868
  42.1 20.0 %all-to-all-start.1 = ((bf16[128,8,256]{0,2,1:T(8,128)(2,1)}), bf16[128,8,256]{0,2,1:T(8,128)(2,1)S(1)}, u32[]{:S(2)}, u32[]{:S(2)}) async-start(bf16[128,8,256]{0,2,1:T(8,128)(2,1)} %bitcast.30), calls=%async_computation.2 | async-start | bytes 1048576 | tf_op jit(solution)/shard_map/all_to_all | solution.py:81
  46.7 5.0 %collective-permute-start = (bf16[4,2048]{1,0:T(4,128)(2,1)S(1)}, bf16[4,2048]{1,0:T(4,128)(2,1)S(1)}, u32[]{:S(2)}, u32[]{:S(2)}) collective-permute-start(bf16[4,2048]{1,0:T(4,128)(2,1)S(1)} %get-tuple-element.54), channel_id=1, source_target_pairs={{0,1},{1,2},{2,3},{3,4},{4,5},{5,6},{6,7},{8,9},{9,10},{10,11},{11... | collective-permute-start | bytes 49160 | tf_op jit(solution)/shard_map/ppermute | solution.py:18
  49.1 4.2 %collective-permute-start.1 = (bf16[4,2048]{1,0:T(4,128)(2,1)S(1)}, bf16[4,2048]{1,0:T(4,128)(2,1)S(1)}, u32[]{:S(2)}, u32[]{:S(2)}) collective-permute-start(bf16[4,2048]{1,0:T(4,128)(2,1)S(1)} %get-tuple-element.53), channel_id=1, source_target_pairs={{1,0},{2,1},{3,2},{4,3},{5,4},{6,5},{7,6},{9,8},{10,9},{11,10},{12... | collective-permute-start | bytes 49160 | tf_op jit(solution)/shard_map/ppermute | solution.py:20
  108.6 19.9 %copy-start.23 = (bf16[16,16,8,128]{3,2,1,0:T(8,128)(2,1)S(1)}, bf16[16,16,8,128]{3,2,1,0:T(8,128)(2,1)}, u32[]{:S(2)}) copy-start(bf16[16,16,8,128]{3,2,1,0:T(8,128)(2,1)} %get-tuple-element.51) | copy-start | bytes 1572868
  128.4 2.0 copy-start.6
  128.4 2.0 copy-start.8
  128.5 2.0 copy-start.4
  128.5 3.4 copy-start.11
  128.5 4.6 %copy-start.10 = (bf16[16,128,1,128]{3,2,1,0:T(2,128)(2,1)}, bf16[16,128,1,128]{3,2,1,0:T(2,128)(2,1)S(1)}, u32[]{:S(2)}) copy-start(bf16[16,128,1,128]{3,2,1,0:T(2,128)(2,1)S(1)} %get-tuple-element.22) | copy-start | bytes 1572868
  128.5 5.1 %copy-start.2 = (bf16[16,128,1,128]{3,2,1,0:T(2,128)(2,1)}, bf16[16,128,1,128]{3,2,1,0:T(2,128)(2,1)S(1)}, u32[]{:S(2)}) copy-start(bf16[16,128,1,128]{3,2,1,0:T(2,128)(2,1)S(1)} %get-tuple-element.21) | copy-start | bytes 1572868
  128.5 6.1 %copy-start = (bf16[16,128,1,128]{3,2,1,0:T(2,128)(2,1)}, bf16[16,128,1,128]{3,2,1,0:T(2,128)(2,1)S(1)}, u32[]{:S(2)}) copy-start(bf16[16,128,1,128]{3,2,1,0:T(2,128)(2,1)S(1)} %get-tuple-element.20) | copy-start | bytes 1572868
  128.5 7.6 %copy-start.14 = (bf16[16,128,1,128]{3,2,1,0:T(2,128)(2,1)}, bf16[16,128,1,128]{3,2,1,0:T(2,128)(2,1)S(1)}, u32[]{:S(2)}) copy-start(bf16[16,128,1,128]{3,2,1,0:T(2,128)(2,1)S(1)} %get-tuple-element.18) | copy-start | bytes 1572868
  128.5 1.4 copy-start.22
  129.9 1.4 copy-start.21
  131.3 1.2 copy-start.20
  133.0 1.0 copy-start.19
  134.1 1.0 copy-start.18
  135.6 1.2 copy-start.25
  135.6 1.3 copy-start.27
  138.9 14.8 %collective-permute-start.2 = (bf16[4,2048]{0,1:T(8,128)(2,1)}, bf16[4,2048]{0,1:T(8,128)(2,1)}, u32[]{:S(2)}, u32[]{:S(2)}) collective-permute-start(bf16[4,2048]{0,1:T(8,128)(2,1)} %copy.145), channel_id=1, source_target_pairs={{1,0},{2,1},{3,2},{4,3},{5,4},{6,5},{7,6},{9,8},{10,9},{11,10},{12... | collective-permute-start | bytes 49160 | tf_op jit(solution)/shard_map/ppermute | solution.py:20
  141.3 12.4 %collective-permute-start.3 = (bf16[4,2048]{0,1:T(8,128)(2,1)}, bf16[4,2048]{0,1:T(8,128)(2,1)}, u32[]{:S(2)}, u32[]{:S(2)}) collective-permute-start(bf16[4,2048]{0,1:T(8,128)(2,1)} %copy.155), channel_id=1, source_target_pairs={{0,1},{1,2},{2,3},{3,4},{4,5},{5,6},{6,7},{8,9},{9,10},{10,11},{11... | collective-permute-start | bytes 49160 | tf_op jit(solution)/shard_map/ppermute | solution.py:18
  148.8 22.7 %all-to-all-start = ((bf16[128,8,256]{0,2,1:T(8,128)(2,1)}), bf16[128,8,256]{0,2,1:T(8,128)(2,1)S(1)}, u32[]{:S(2)}, u32[]{:S(2)}) async-start(bf16[128,8,256]{0,2,1:T(8,128)(2,1)} %bitcast.28), calls=%async_computation.1 | async-start | bytes 1048576 | tf_op jit(solution)/shard_map/all_to_all | solution.py:82
  153.5 84.4 %all-reduce.4.cloned.1.call-start = ((), (), s32[]{:S(2)}) async-start(), calls=%async_computation.6 | async-start | bytes 2359296 | tf_op jit(solution)/shard_map/psum | solution.py:115
  153.7 6.9 %copy-start.9 = (bf16[16,128,1,128]{3,2,1,0:T(2,128)(2,1)S(1)}, bf16[16,128,1,128]{3,2,1,0:T(2,128)(2,1)}, u32[]{:S(2)}) copy-start(bf16[16,128,1,128]{3,2,1,0:T(2,128)(2,1)} %copy-done.8) | copy-start | bytes 1572868
  160.6 1.2 copy-start.7
  161.8 1.2 copy-start.5
  163.1 1.2 copy-start.12
  163.1 1.5 copy-start.13
  164.6 1.2 copy-start.3
  165.8 1.2 copy-start.1
  167.4 1.2 copy-start.15
  173.9 1.4 copy-start.28
  182.3 1.0 copy-start.17
  182.4 195.3 %reduce-scatter.2.cloned.1.call-start = ((), (), s32[]{:S(2)}) async-start(), calls=%async_computation.5 | async-start | bytes 2162688 | tf_op jit(solution)/shard_map/reduce_scatter | solution.py:130
  183.8 1.9 copy-start.24
Sparse Core Ops, SparseCore 0:
  9.9 29.3 all-gather.2
  41.1 57.0 all-gather.4
  182.5 55.3 all-reduce.3
  240.7 136.9 reduce-scatter.1
where the time goes:
time: 386 us; the launch traced here: 384 us
  waiting for transfers between devices  223 us (58%)
  local copies, waits for them, and re-layouts  59.2 us (15%)
  blocking collectives  39.9 us (10%)
  matrix products  18.8 us (5%)
  starting transfers between devices  18.4 us (5%)
  between operations  14.4 us (4%)
  other arithmetic  10.6 us (3%)
    reduce_scatter x1, waiting for transfers between devices, body(): lax.psum_scatter(table_term, ('fsdp', 'seq'), scatter_dimension=0, tiled=...  137 us
    unnamed x1, blocking collectives  39.9 us
    all_gather x1, waiting for transfers between devices, body(): lax.all_gather(kernel, 'fsdp', axis=0, tiled=True)  34.5 us
    all_gather x1, waiting for transfers between devices, body(): table = lax.all_gather(type_table, 'fsdp', axis=0, tiled=True)  30.6 us
    slice x1, local copies, waits for them, and re-layouts, body(): weights[:, :, k, :]  19.8 us
    unnamed x66, local copies, waits for them, and re-layouts  17.4 us
    psum x1, waiting for transfers between devices, body(): kernel_grad = lax.psum(kernel_part, 'fsdp')  11.7 us
    reshape x1, local copies, waits for them, and re-layouts, body(): lax.all_gather(kernel, 'fsdp', axis=0, tiled=True)  10.5 us
  transfers between devices with their start and end apart: 10, of which 6 were waited for; matrix products, arithmetic and copies ran while one was open for 8% of the time, Pallas kernels for 0%

commit v1 on v0

--- a/solution.py
+++ b/solution.py
@@ -112,7 +112,7 @@
             )
         )
     kernel_part = jnp.stack(kterms, axis=2).reshape(slice_width, KERNEL * chans) * scale
-    kernel_grad = lax.psum(kernel_part, "fsdp")
+    kernel_grad = jnp.sum(lax.all_gather(kernel_part, "fsdp"), axis=0)
     dnormed = dnormed.reshape(length, width)
     gain_term = jnp.sum(dnormed * mixed * inv, axis=0) * scale
     scaled = norm_gain * dnormed

time: 386 us -> 369 us (0.956)
  waiting for transfers between devices: 223 us -> 206 us
  local copies, waits for them, and re-layouts: 59.2 us -> 51.8 us
  blocking collectives: 39.9 us -> 46.3 us
    reduce_scatter x1, waiting for transfers between devices: 137 us -> 118 us  [body(): lax.psum_scatter(table_term, ('fsdp', 'seq'), scatter_dimension=0, tiled=...]
    all_to_all x1, waiting for transfers between devices: 0.01 us -> 13.5 us  [body(): lax.all_to_all(dflat, 'seq', split_axis=1, concat_axis=0, tiled=True)]
    psum x1 -> x0, waiting for transfers between devices: 11.7 us -> none  [body(): kernel_grad = lax.psum(kernel_part, 'fsdp')]
    all_gather x1, waiting for transfers between devices: 34.5 us -> 42 us  [body(): lax.all_gather(kernel, 'fsdp', axis=0, tiled=True)]
    unnamed x1, blocking collectives: 39.9 us -> 46.3 us
    all_to_all x1, waiting for transfers between devices: 6.03 us -> 0.01 us  [body(): lax.all_to_all(normed, 'seq', split_axis=1, concat_axis=0, tiled=True)]
    unnamed x66 -> x70, local copies, waits for them, and re-layouts: 17.4 us -> 12.6 us
  transfers between devices with their start and end apart: 10 -> 10, of which waited for: 6 -> 5; matrix products, arithmetic and copies ran while one was open for 8% -> 17% of each run, Pallas kernels for 0% -> 0%
where the time goes in v1:
time: 369 us; the launch traced here: 367 us
  waiting for transfers between devices  206 us (56%)
  local copies, waits for them, and re-layouts  51.8 us (14%)
  blocking collectives  46.3 us (13%)
  starting transfers between devices  19.5 us (5%)
  matrix products  15.5 us (4%)
  between operations  14.4 us (4%)
  other arithmetic  13.3 us (4%)
    reduce_scatter x1, waiting for transfers between devices, body(): lax.psum_scatter(table_term, ('fsdp', 'seq'), scatter_dimension=0, tiled=...  118 us
    unnamed x1, blocking collectives  46.3 us
    all_gather x1, waiting for transfers between devices, body(): lax.all_gather(kernel, 'fsdp', axis=0, tiled=True)  42 us
    all_gather x1, waiting for transfers between devices, body(): table = lax.all_gather(type_table, 'fsdp', axis=0, tiled=True)  30.6 us
    slice x1, local copies, waits for them, and re-layouts, body(): weights[:, :, k, :]  19.9 us
    all_to_all x1, waiting for transfers between devices, body(): lax.all_to_all(dflat, 'seq', split_axis=1, concat_axis=0, tiled=True)  13.5 us
    unnamed x70, local copies, waits for them, and re-layouts  12.6 us
    reshape x1, local copies, waits for them, and re-layouts, body(): lax.all_gather(kernel, 'fsdp', axis=0, tiled=True)  10.5 us
  transfers between devices with their start and end apart: 10, of which 5 were waited for; matrix products, arithmetic and copies ran while one was open for 17% of the time, Pallas kernels for 0%

profile of v1, /device:TPU:0, one launch (start us, length us, event | category | flops | bytes accessed | tf_op | source)
XLA Modules:
  0.0 367.2 jit_solution(5028256366065421682)
XLA Ops:
  7.2 0.7 all-gather.4.cloned.1.call-update
  8.0 0.7 all-gather.6.cloned.1.call-update
  8.7 30.6 %all-gather.4.cloned.1.call-done = bf16[256,2048]{1,0:T(8,128)(2,1)} async-done(((bf16[64,2048]{1,0:T(8,128)(2,1)}), bf16[256,2048]{1,0:T(8,128)(2,1)}) %all-gather.4.cloned.1.call-update) | async-done | bytes 1048592 | tf_op jit(solution)/shard_map/all_gather | solution.py:41
  39.2 1.7 multiply_reduce_fusion.2
  41.1 1.7 collective-permute-start
  42.9 1.3 collective-permute-start.1
  44.3 1.2 copy.216
  45.4 1.0 copy.192
  46.4 7.1 %all-to-all-start.1 = ((bf16[128,8,256]{0,2,1:T(8,128)(2,1)}), bf16[128,8,256]{0,2,1:T(8,128)(2,1)S(1)}, u32[]{:S(2)}, u32[]{:S(2)}) async-start(bf16[128,8,256]{0,2,1:T(8,128)(2,1)} %bitcast.30), calls=%async_computation.2 | async-start | bytes 1048576 | tf_op jit(solution)/shard_map/all_to_all | solution.py:81
  53.6 2.6 fusion.52
  56.2 42.0 %all-gather.6.cloned.1.call-done = bf16[2048,1152]{1,0:T(8,128)(2,1)} async-done(((bf16[512,1152]{1,0:T(8,128)(2,1)}), bf16[2048,1152]{1,0:T(8,128)(2,1)}) %all-gather.6.cloned.1.call-update) | async-done | bytes 4718608 | tf_op jit(solution)/shard_map/all_gather | solution.py:52
  98.2 10.5 %reshape.99 = bf16[16,128,9,128]{3,2,1,0:T(8,128)(2,1)} reshape(bf16[2048,1152]{1,0:T(8,128)(2,1)} %all-gather.6.cloned.1.call-done) | data formatting | bytes 9437184 | tf_op jit(solution)/shard_map/reshape | solution.py:52
  108.6 19.9 %fusion.82 = (bf16[16,128,1,128]{3,2,1,0:T(2,128)(2,1)S(1)}, bf16[16,128,1,128]{3,2,1,0:T(2,128)(2,1)S(1)}, bf16[16,128,1,128]{3,2,1,0:T(2,128)(2,1)S(1)}, bf16[...) fusion(bf16[16,128,9,128]{3,2,1,0:T(8,128)(2,1)} %reshape.99), kind=kLoop, calls=%fused_computation.153 | loop fusion | bytes 9437184 | tf_op jit(solution)/shard_map/slice | solution.py:60
  129.1 0.9 copy-done.25
  130.6 0.9 copy-done.24
  132.0 0.9 copy-done.23
  133.4 0.5 convolution_add_fusion.12
  134.9 0.5 convolution_add_fusion.10
  135.5 0.5 convolution_add_fusion.9
  136.0 0.7 copy-done.28
  136.8 0.8 fusion.14
  137.7 1.0 copy.142
  138.7 4.6 %all-to-all-start = ((bf16[128,8,256]{0,2,1:T(8,128)(2,1)}), bf16[128,8,256]{0,2,1:T(8,128)(2,1)S(1)}, u32[]{:S(2)}, u32[]{:S(2)}) async-start(bf16[128,8,256]{0,2,1:T(8,128)(2,1)} %bitcast.28), calls=%async_computation.1 | async-start | bytes 1048576 | tf_op jit(solution)/shard_map/all_to_all | solution.py:82
  144.1 1.0 copy.167
  145.1 13.5 %all-to-all-done = bf16[128,8,256]{0,2,1:T(8,128)(2,1)S(1)} async-done(((bf16[128,8,256]{0,2,1:T(8,128)(2,1)}), bf16[128,8,256]{0,2,1:T(8,128)(2,1)S(1)}, u32[]{:S(2)}, u32[]{:S(2)}) %all-to-all-start) | async-done | bytes 524320 | tf_op jit(solution)/shard_map/all_to_all | solution.py:82
  159.2 1.4 fusion.10
  163.2 0.7 copy.193
  164.0 1.2 reshape.98
  165.3 0.9 slice_bitcast_fusion
  166.5 1.3 collective-permute-start.2
  167.8 1.1 copy.153
  168.9 3.1 collective-permute-start.3
  172.0 0.5 fusion.63
  172.5 1.2 collective-permute-done.3
  173.7 5.9 %pad_maximum_fusion = (bf16[128,2048]{0,1:T(8,128)(2,1)S(1)}, bf16[128,2048]{0,1:T(8,128)(2,1)S(1)}, bf16[128,2048]{0,1:T(8,128)(2,1)S(1)}, bf16[128,2048]{0,1:T...) fusion(bf16[128,2048]{0,1:T(8,128)(2,1)} %bitcast.13, ...), kind=kLoop, calls=%fused_computation.104 | loop fusion | flops 8388608 | bytes 4751360 | tf_op jit(solution)/shard_map/concatenate | solution.py:16
  180.0 0.8 copy-done.9
  181.2 0.9 copy-done.7
  182.4 0.9 copy-done.15
  183.6 0.9 copy-done.5
  184.9 0.9 copy-done.3
  186.1 0.9 copy-done.1
  187.3 0.9 copy-done.17
  189.2 0.7 copy-done.21
  190.3 1.9 convolution_multiply_fusion
  192.3 46.3 %all-reduce.1 = f32[2048]{0:T(1024)S(1)} all-reduce(f32[2048]{0:T(1024)S(1)} %broadcast_multiply_fusion.1), channel_id=3, replica_groups=mesh['fsdp'=4,'seq'=8] {'fsdp','seq'}, use_global_device_ids=true, to_apply=%region_4.5.clone | all-reduce | flops 2048 | bytes 16384
  238.6 0.6 dynamic-slice
  239.2 3.7 %reduce_sum.39 = f32[256,1152]{1,0:T(8,128)} reduce(f32[4,256,1152]{2,1,0:T(8,128)} %all-gather.8.cloned.1.call-done, f32[]{:T(128)} %constant.6.clone.1), dimensions={0}, to_apply=%region_5.6 | reduce | flops 884736 | bytes 5898244 | tf_op jit(solution)/shard_map/reduce_sum | solution.py:115
  242.9 117.8 %reduce-scatter.2.cloned.1.call-done = f32[8,2048]{1,0:T(8,128)} async-done(((f32[256,2048]{1,0:T(8,128)}), f32[8,2048]{1,0:T(8,128)}) %reduce-scatter.2.cloned.1.call-update) | async-done | bytes 65552 | tf_op jit(solution)/shard_map/reduce_scatter | solution.py:130
  (103 shorter events, 11.7 us)
Async XLA Ops:
  7.2 32.1 %copy-start.33 = (s32[1,128]{1,0:T(1,128)S(1)}, s32[1,128]{1,0:T(1,128)}, u32[]{:S(2)}) copy-start(s32[1,128]{1,0:T(1,128)} %param.7) | copy-start | bytes 1540
  7.2 32.1 %copy-start.29 = (bf16[1,128,2048]{2,1,0:T(8,128)(2,1)S(1)}, bf16[1,128,2048]{2,1,0:T(8,128)(2,1)}, u32[]{:S(2)}) copy-start(bf16[1,128,2048]{2,1,0:T(8,128)(2,1)} %param.6) | copy-start | bytes 1572868
  7.2 32.0 %all-gather.4.cloned.1.call-start = ((), (), s32[]{:S(2)}) async-start(), calls=%async_computation.3 | async-start | bytes 1310720 | tf_op jit(solution)/shard_map/all_gather | solution.py:41
  7.9 90.2 %all-gather.6.cloned.1.call-start = ((), (), s32[]{:S(2)}) async-start(), calls=%async_computation.4 | async-start | bytes 5898240 | tf_op jit(solution)/shard_map/all_gather | solution.py:52
  39.2 1.7 copy-start.32
  40.9 3.3 copy-start.20
  41.1 12.5 %collective-permute-start = (bf16[4,2048]{1,0:T(4,128)(2,1)S(1)}, bf16[4,2048]{1,0:T(4,128)(2,1)S(1)}, u32[]{:S(2)}, u32[]{:S(2)}) collective-permute-start(bf16[4,2048]{1,0:T(4,128)(2,1)S(1)} %get-tuple-element.46), channel_id=1, source_target_pairs={{0,1},{1,2},{2,3},{3,4},{4,5},{5,6},{6,7},{8,9},{9,10},{10,11},{11... | collective-permute-start | bytes 49160 | tf_op jit(solution)/shard_map/ppermute | solution.py:18
  42.9 10.7 %collective-permute-start.1 = (bf16[4,2048]{1,0:T(4,128)(2,1)S(1)}, bf16[4,2048]{1,0:T(4,128)(2,1)S(1)}, u32[]{:S(2)}, u32[]{:S(2)}) collective-permute-start(bf16[4,2048]{1,0:T(4,128)(2,1)S(1)} %get-tuple-element.45), channel_id=1, source_target_pairs={{1,0},{2,1},{3,2},{4,3},{5,4},{6,5},{7,6},{9,8},{10,9},{11,10},{12... | collective-permute-start | bytes 49160 | tf_op jit(solution)/shard_map/ppermute | solution.py:20
  46.4 92.3 %all-to-all-start.1 = ((bf16[128,8,256]{0,2,1:T(8,128)(2,1)}), bf16[128,8,256]{0,2,1:T(8,128)(2,1)S(1)}, u32[]{:S(2)}, u32[]{:S(2)}) async-start(bf16[128,8,256]{0,2,1:T(8,128)(2,1)} %bitcast.30), calls=%async_computation.2 | async-start | bytes 1048576 | tf_op jit(solution)/shard_map/all_to_all | solution.py:81
  108.6 20.0 %copy-start.26 = (bf16[16,16,8,128]{3,2,1,0:T(8,128)(2,1)S(1)}, bf16[16,16,8,128]{3,2,1,0:T(8,128)(2,1)}, u32[]{:S(2)}) copy-start(bf16[16,16,8,128]{3,2,1,0:T(8,128)(2,1)} %get-tuple-element.43) | copy-start | bytes 1572868
  128.5 2.0 copy-start.8
  128.5 2.0 copy-start.6
  128.6 3.4 copy-start.10
  128.6 3.4 copy-start.14
  128.6 4.8 %copy-start.12 = (bf16[16,128,1,128]{3,2,1,0:T(2,128)(2,1)}, bf16[16,128,1,128]{3,2,1,0:T(2,128)(2,1)S(1)}, u32[]{:S(2)}) copy-start(bf16[16,128,1,128]{3,2,1,0:T(2,128)(2,1)S(1)} %get-tuple-element.14) | copy-start | bytes 1572868
  128.6 5.4 %copy-start.4 = (bf16[16,128,1,128]{3,2,1,0:T(2,128)(2,1)}, bf16[16,128,1,128]{3,2,1,0:T(2,128)(2,1)S(1)}, u32[]{:S(2)}) copy-start(bf16[16,128,1,128]{3,2,1,0:T(2,128)(2,1)S(1)} %get-tuple-element.13) | copy-start | bytes 1572868
  128.6 6.3 %copy-start.2 = (bf16[16,128,1,128]{3,2,1,0:T(2,128)(2,1)}, bf16[16,128,1,128]{3,2,1,0:T(2,128)(2,1)S(1)}, u32[]{:S(2)}) copy-start(bf16[16,128,1,128]{3,2,1,0:T(2,128)(2,1)S(1)} %get-tuple-element.12) | copy-start | bytes 1572868
  128.6 6.8 %copy-start = (bf16[16,128,1,128]{3,2,1,0:T(2,128)(2,1)}, bf16[16,128,1,128]{3,2,1,0:T(2,128)(2,1)S(1)}, u32[]{:S(2)}) copy-start(bf16[16,128,1,128]{3,2,1,0:T(2,128)(2,1)S(1)} %get-tuple-element.11) | copy-start | bytes 1572868
  128.6 7.4 %copy-start.16 = (bf16[16,128,1,128]{3,2,1,0:T(2,128)(2,1)}, bf16[16,128,1,128]{3,2,1,0:T(2,128)(2,1)S(1)}, u32[]{:S(2)}) copy-start(bf16[16,128,1,128]{3,2,1,0:T(2,128)(2,1)S(1)} %get-tuple-element.10) | copy-start | bytes 1572868
  128.6 1.4 copy-start.25
  130.1 1.4 copy-start.24
  131.5 1.4 copy-start.23
  133.4 1.0 copy-start.22
  135.4 1.2 copy-start.28
  135.5 1.3 copy-start.30
  137.7 5.9 %copy-start.18 = (bf16[128,16,128]{2,0,1:T(8,128)(2,1)}, bf16[128,16,128]{2,0,1:T(8,128)(2,1)S(1)}, u32[]{:S(2)}) copy-start(bf16[128,16,128]{2,0,1:T(8,128)(2,1)S(1)} %fusion.14) | copy-start | bytes 1572868
  138.7 20.0 %all-to-all-start = ((bf16[128,8,256]{0,2,1:T(8,128)(2,1)}), bf16[128,8,256]{0,2,1:T(8,128)(2,1)S(1)}, u32[]{:S(2)}, u32[]{:S(2)}) async-start(bf16[128,8,256]{0,2,1:T(8,128)(2,1)} %bitcast.28), calls=%async_computation.1 | async-start | bytes 1048576 | tf_op jit(solution)/shard_map/all_to_all | solution.py:82
  143.3 95.9 %all-gather.8.cloned.1.call-start = ((), (), s32[]{:S(2)}) async-start(), calls=%async_computation.6 | async-start | bytes 5898240 | tf_op jit(solution)/shard_map/all_gather | solution.py:115
  159.0 1.6 copy-start.31
  165.2 6.7 %copy-start.13 = (bf16[16,128,1,128]{3,2,1,0:T(2,128)(2,1)S(1)}, bf16[16,128,1,128]{3,2,1,0:T(2,128)(2,1)}, u32[]{:S(2)}) copy-start(bf16[16,128,1,128]{3,2,1,0:T(2,128)(2,1)} %copy-done.12) | copy-start | bytes 1572868
  165.2 6.8 %copy-start.19 = (bf16[128,16,128]{2,0,1:T(8,128)(2,1)S(1)}, bf16[128,16,128]{2,0,1:T(8,128)(2,1)}, u32[]{:S(2)}) copy-start(bf16[128,16,128]{2,0,1:T(8,128)(2,1)} %copy-done.18) | copy-start | bytes 1572868
  165.2 195.5 %reduce-scatter.2.cloned.1.call-start = ((), (), s32[]{:S(2)}) async-start(), calls=%async_computation.5 | async-start | bytes 2162688 | tf_op jit(solution)/shard_map/reduce_scatter | solution.py:130
  166.5 6.0 %collective-permute-start.2 = (bf16[4,2048]{0,1:T(8,128)(2,1)S(1)}, bf16[4,2048]{0,1:T(8,128)(2,1)}, u32[]{:S(2)}, u32[]{:S(2)}) collective-permute-start(bf16[4,2048]{0,1:T(8,128)(2,1)S(1)} %copy.143), channel_id=1, source_target_pairs={{1,0},{2,1},{3,2},{4,3},{5,4},{6,5},{7,6},{9,8},{10,9},{11,10},{12... | collective-permute-start | bytes 49160 | tf_op jit(solution)/shard_map/ppermute | solution.py:20
  168.9 4.8 %collective-permute-start.3 = (bf16[4,2048]{0,1:T(8,128)(2,1)}, bf16[4,2048]{0,1:T(8,128)(2,1)S(1)}, u32[]{:S(2)}, u32[]{:S(2)}) collective-permute-start(bf16[4,2048]{0,1:T(8,128)(2,1)} %copy.153), channel_id=1, source_target_pairs={{0,1},{1,2},{2,3},{3,4},{4,5},{5,6},{6,7},{8,9},{9,10},{10,11},{11... | collective-permute-start | bytes 49160 | tf_op jit(solution)/shard_map/ppermute | solution.py:18
  173.7 5.9 %copy-start.11 = (bf16[16,128,1,128]{3,2,1,0:T(2,128)(2,1)S(1)}, bf16[16,128,1,128]{3,2,1,0:T(2,128)(2,1)}, u32[]{:S(2)}) copy-start(bf16[16,128,1,128]{3,2,1,0:T(2,128)(2,1)} %copy-done.10) | copy-start | bytes 1572868
  179.6 1.2 copy-start.9
  180.8 1.2 copy-start.7
  182.0 1.2 copy-start.15
  183.3 1.2 copy-start.5
  184.5 1.2 copy-start.3
  185.7 1.2 copy-start.1
  186.9 1.2 copy-start.17
  188.9 1.0 copy-start.21
  190.3 1.9 copy-start.27
Sparse Core Ops, SparseCore 0:
  9.9 29.3 all-gather.3
  41.1 57.0 all-gather.5
  165.4 55.6 all-gather.7
  223.8 136.8 reduce-scatter.1
